TPU v7x, 32 devices: a whole 2x2x4 slice. The times are simulated.
32 devices in a mesh: dp: 16 (over z, x, core), group: 2 (over y).
Axes of the slice: x: 2, y: 2, z: 4, core: 2. Of those that a mesh axis runs over, the one named last changes fastest.
Arguments:
- inputs: bfloat16 [32768, 2048], P('dp', 'group'), may hold values from -6 to 6
- grad_out: bfloat16 [32768, 2048], P(('dp', 'group')), may hold values from -0.0625 to 0.0625
- weight: bfloat16 [2048, 2048], P('group'), may hold values from -6 to 6
- old_basis: float32 [2048, 256], P('group'), may hold values from -0.125 to 0.125
- first_moment: float32 [256, 2048], P(None, 'dp'), may hold values from -6 to 6
- second_moment: float32 [256, 2048], P(None, 'dp'), may hold values from 0.1 to 3
Outputs:
- new_weight: bfloat16 [2048, 2048], P('group')
- new_first: float32 [256, 2048], P(None, 'dp')
- new_second: float32 [256, 2048], P(None, 'dp')
- new_basis: float32 [2048, 256], P('group')
All inputs are finite; a program needn't handle non-finite values.
Results may differ from a plain program's by a relative error of at most 0.011.
Values may be sent and summed in bfloat16 or wider, within the bound.
No kernel may reach another device: no remote copies, remote signals or barrier semaphores. Data moves between devices by JAX's collectives and lax.ppermute only.
A program may use at most 64 MiB of HBM per device.

v0:
```python
import jax
import jax.numpy as jnp
from jax import lax
from jax.sharding import PartitionSpec as P

NS_STEPS = 5
STEP = 10
BETA_ONE = 0.9
BETA_TWO = 0.99
ADAM_EPS = 1e-08
HIGHEST = lax.Precision.HIGHEST


def matmul(left, right):
    return jnp.dot(left, right, precision=HIGHEST)


def inner_gram(matrix):
    return lax.dot_general(matrix, matrix, (((0,), (0,)), ((), ())), precision=HIGHEST)


def refine_group(subspace):
    squares = lax.psum(jnp.sum(subspace * subspace), "group")
    iterate = subspace / jnp.sqrt(squares)
    for sweep in range(NS_STEPS):
        gram = lax.psum(inner_gram(iterate).astype(jnp.bfloat16), "group").astype(jnp.float32)
        iterate = 1.5 * iterate - 0.5 * matmul(iterate, gram)
    return iterate


def shards(inputs, grad_out, weight, old_basis, first_moment, second_moment):
    partial_grad = lax.dot_general(
        inputs,
        lax.all_gather(grad_out, "group", axis=0, tiled=True),
        (((0,), (0,)), ((), ())),
        preferred_element_type=jnp.float32,
    )
    grad_block = lax.psum_scatter(partial_grad, "dp", scatter_dimension=1, tiled=True)
    projected = lax.psum(matmul(old_basis.T, grad_block).astype(jnp.bfloat16), "group").astype(
        jnp.float32
    )
    new_first = BETA_ONE * first_moment + (1.0 - BETA_ONE) * projected
    new_second = BETA_TWO * second_moment + (1.0 - BETA_TWO) * projected * projected
    direction = (
        new_first
        / (1.0 - BETA_ONE**STEP)
        / (jnp.sqrt(new_second / (1.0 - BETA_TWO**STEP)) + ADAM_EPS)
    )
    col_count = grad_block.shape[1]
    col_offset = lax.axis_index("dp") * col_count
    own_cols = lax.dynamic_slice_in_dim(weight, col_offset, col_count, 1).astype(jnp.float32)
    updated = (own_cols - matmul(old_basis, direction)).astype(jnp.bfloat16)
    new_weight = lax.all_gather(updated, "dp", axis=1, tiled=True)
    subspace_terms = matmul(grad_block, projected.T)
    subspace = lax.psum(subspace_terms, "dp")
    new_basis = refine_group(subspace)
    return (new_weight, new_first, new_second, new_basis)


def solution(mesh):
    return jax.shard_map(
        shards,
        mesh=mesh,
        in_specs=(
            P("dp", "group"),
            P(("dp", "group"), None),
            P("group", None),
            P("group", None),
            P(None, "dp"),
            P(None, "dp"),
        ),
        out_specs=(P("group", None), P(None, "dp"), P(None, "dp"), P("group", None)),
        check_vma=False,
    )
```

profile of v0, /device:TPU:0, one launch (start us, length us, event | category | flops | bytes accessed | tf_op | source)
XLA Modules:
  0.0 558.3 jit_solution(406713574473706663)
XLA Ops:
  8.0 108.3 %all-gather.3.cloned.1.call-done = bf16[2048,2048]{1,0:T(8,128)(2,1)} async-done(((bf16[1024,2048]{1,0:T(8,128)(2,1)}), bf16[2048,2048]{1,0:T(8,128)(2,1)}) %all-gather.3.cloned.1.call-update) | async-done | bytes 8388624 | tf_op jit(solution)/shard_map/all_gather | solution.py:34
  116.3 14.6 %fusion.21 = f32[1024,2048]{1,0:T(8,128)} fusion(bf16[2048,1024]{1,0:T(8,128)(2,1)} %param.6, bf16[2048,2048]{1,0:T(8,128)(2,1)} %all-gather.3.cloned.1.call-done), kind=kOutput, calls=%fused_computation.38 | convolution fusion | flops 8589934592 | bytes 20971520 | tf_op jit(solution)/shard_map/dot_general | solution.py:32
  130.9 103.7 %reduce-scatter.2.cloned.1.call-done = f32[1024,128]{1,0:T(8,128)} async-done(((f32[1024,2048]{1,0:T(8,128)}), f32[1024,128]{1,0:T(8,128)}) %reduce-scatter.2.cloned.1.call-update) | async-done | bytes 524304 | tf_op jit(solution)/shard_map/reduce_scatter | solution.py:38
  234.6 2.7 fusion.7
  237.4 20.7 %all-reduce.8.cloned.1.call-done = bf16[256,128]{0,1:T(8,128)(2,1)} async-done(((bf16[256,128]{0,1:T(8,128)(2,1)}), bf16[256,128]{0,1:T(8,128)(2,1)}) %all-reduce.8.cloned.1.call-update) | async-done | bytes 65552 | tf_op jit(solution)/shard_map/psum | solution.py:39
  258.1 2.6 fusion.22
  260.8 95.1 %all-reduce.10.cloned.1.call-done = f32[1024,256]{1,0:T(8,128)} async-done(((f32[1024,256]{1,0:T(8,128)}), f32[1024,256]{1,0:T(8,128)}) %all-reduce.10.cloned.1.call-update) | async-done | bytes 1048592 | tf_op jit(solution)/shard_map/psum | solution.py:55
  355.8 2.2 multiply_reduce_fusion
  358.0 5.5 psum.58
  364.3 4.0 convolution_convert_fusion.4
  368.4 20.7 %all-reduce.12.cloned.1.call-done = bf16[256,256]{1,0:T(8,128)(2,1)} async-done(((bf16[256,256]{1,0:T(8,128)(2,1)}), bf16[256,256]{1,0:T(8,128)(2,1)}) %all-reduce.12.cloned.1.call-update) | async-done | bytes 131088 | tf_op jit(solution)/shard_map/psum | solution.py:26
  389.1 1.6 fusion.4
  390.7 2.5 convolution_convert_fusion.3
  393.5 21.4 %all-reduce.14.cloned.1.call-done = bf16[256,256]{1,0:T(8,128)(2,1)} async-done(((bf16[256,256]{1,0:T(8,128)(2,1)}), bf16[256,256]{1,0:T(8,128)(2,1)}) %all-reduce.14.cloned.1.call-update) | async-done | bytes 131088 | tf_op jit(solution)/shard_map/psum | solution.py:26
  414.9 1.5 fusion.3
  416.4 2.5 convolution_convert_fusion.2
  419.0 1.0 constant_dynamic-slice_fusion
  420.0 0.9 copy.16
  421.0 0.8 copy.12
  421.7 18.9 %all-reduce.16.cloned.1.call-done = bf16[256,256]{1,0:T(8,128)(2,1)} async-done(((bf16[256,256]{1,0:T(8,128)(2,1)}), bf16[256,256]{1,0:T(8,128)(2,1)}) %all-reduce.16.cloned.1.call-update) | async-done | bytes 131088 | tf_op jit(solution)/shard_map/psum | solution.py:26
  440.6 1.5 fusion.2
  442.2 2.5 convolution_convert_fusion.1
  444.7 1.0 fusion.8
  445.7 20.6 %all-reduce.18.cloned.1.call-done = bf16[256,256]{1,0:T(8,128)(2,1)} async-done(((bf16[256,256]{1,0:T(8,128)(2,1)}), bf16[256,256]{1,0:T(8,128)(2,1)}) %all-reduce.18.cloned.1.call-update) | async-done | bytes 131088 | tf_op jit(solution)/shard_map/psum | solution.py:26
  466.4 1.5 fusion.1
  467.9 2.5 convolution_convert_fusion
  470.5 2.9 fusion.6
  473.4 0.8 copy.14
  474.9 17.2 %all-reduce.20.cloned.1.call-done = bf16[256,256]{1,0:T(8,128)(2,1)} async-done(((bf16[256,256]{1,0:T(8,128)(2,1)}), bf16[256,256]{1,0:T(8,128)(2,1)}) %all-reduce.20.cloned.1.call-update) | async-done | bytes 131088 | tf_op jit(solution)/shard_map/psum | solution.py:26
  492.1 2.5 fusion
  494.6 50.5 %all-gather.5.cloned.1.call-done = bf16[1024,2048]{0,1:T(8,128)(2,1)} async-done(((bf16[1024,128]{0,1:T(8,128)(2,1)}), bf16[1024,2048]{0,1:T(8,128)(2,1)}) %all-gather.5.cloned.1.call-update) | async-done | bytes 4194320 | tf_op jit(solution)/shard_map/all_gather | solution.py:53
  545.1 6.4 %copy.13 = bf16[1024,2048]{1,0:T(8,128)(2,1)} copy(bf16[1024,2048]{0,1:T(8,128)(2,1)} %all-gather.5.cloned.1.call-done) | data formatting | bytes 8388608
  (30 shorter events, 2.3 us)
Async XLA Ops:
  7.2 227.5 %copy-start = (f32[1024,256]{1,0:T(8,128)S(1)}, f32[1024,256]{1,0:T(8,128)}, u32[]{:S(2)}) copy-start(f32[1024,256]{1,0:T(8,128)} %param.9) | copy-start | bytes 3145732
  7.2 109.1 %all-gather.3.cloned.1.call-start = ((), (), s32[]{:S(2)}) async-start(), calls=%async_computation.1 | async-start | bytes 12582912 | tf_op jit(solution)/shard_map/all_gather | solution.py:34
  7.9 226.7 %reduce-scatter.2.cloned.1.call-start = ((), (), s32[]{:S(2)}) async-start(), calls=%async_computation.2 | async-start | bytes 8912896 | tf_op jit(solution)/shard_map/reduce_scatter | solution.py:38
  130.9 127.2 %all-reduce.8.cloned.1.call-start = ((), (), s32[]{:S(2)}) async-start(), calls=%async_computation.3 | async-start | bytes 131072 | tf_op jit(solution)/shard_map/psum | solution.py:39
  237.4 118.5 %all-reduce.10.cloned.1.call-start = ((), (), s32[]{:S(2)}) async-start(), calls=%async_computation.5 | async-start | bytes 2097152 | tf_op jit(solution)/shard_map/psum | solution.py:55
  260.7 128.4 %all-reduce.12.cloned.1.call-start = ((), (), s32[]{:S(2)}) async-start(), calls=%async_computation.6 | async-start | bytes 262144 | tf_op jit(solution)/shard_map/psum | solution.py:26
  355.8 33.3 %copy-start.1 = (f32[1024,256]{1,0:T(8,128)S(1)}, f32[1024,256]{1,0:T(8,128)}, u32[]{:S(2)}) copy-start(f32[1024,256]{1,0:T(8,128)} %all-reduce.10.cloned.1.call-done) | copy-start | bytes 3145732
  368.3 46.6 %all-reduce.14.cloned.1.call-start = ((), (), s32[]{:S(2)}) async-start(), calls=%async_computation.7 | async-start | bytes 262144 | tf_op jit(solution)/shard_map/psum | solution.py:26
  390.7 30.2 %copy-start.2 = (f32[256,128]{1,0:T(8,128)S(1)}, f32[256,128]{1,0:T(8,128)}, u32[]{:S(2)}) copy-start(f32[256,128]{1,0:T(8,128)} %param.10) | copy-start | bytes 393220
  390.7 30.3 %copy-start.3 = (f32[256,128]{1,0:T(8,128)S(1)}, f32[256,128]{1,0:T(8,128)}, u32[]{:S(2)}) copy-start(f32[256,128]{1,0:T(8,128)} %param.11) | copy-start | bytes 393220
  393.2 47.4 %all-reduce.16.cloned.1.call-start = ((), (), s32[]{:S(2)}) async-start(), calls=%async_computation.8 | async-start | bytes 262144 | tf_op jit(solution)/shard_map/psum | solution.py:26
  419.0 47.4 %all-reduce.18.cloned.1.call-start = ((), (), s32[]{:S(2)}) async-start(), calls=%async_computation.9 | async-start | bytes 262144 | tf_op jit(solution)/shard_map/psum | solution.py:26
  444.7 47.4 %all-reduce.20.cloned.1.call-start = ((), (), s32[]{:S(2)}) async-start(), calls=%async_computation.10 | async-start | bytes 262144 | tf_op jit(solution)/shard_map/psum | solution.py:26
  470.4 74.7 %all-gather.5.cloned.1.call-start = ((), (), s32[]{:S(2)}) async-start(), calls=%async_computation.4 | async-start | bytes 4456448 | tf_op jit(solution)/shard_map/all_gather | solution.py:53
Sparse Core Ops, SparseCore 0:
  9.5 106.6 all-gather.2
  131.0 103.5 reduce-scatter.1
  237.5 20.5 all-reduce.7
  262.0 93.7 all-reduce.9
  368.4 20.6 all-reduce.11
  393.4 21.5 all-reduce.13
  419.1 21.5 all-reduce.15
  444.8 21.5 all-reduce.17
  470.5 21.5 all-reduce.19
  494.7 50.3 all-gather.4
where the time goes:
time: 559 us; the launch traced here: 558 us
  waiting for transfers between devices  478 us (86%)
  matrix products  45.4 us (8%)
  between operations  15 us (3%)
  local copies, waits for them, and re-layouts  10.6 us (2%)
    all_gather x1, waiting for transfers between devices, shards(): lax.all_gather(grad_out, 'group', axis=0, tiled=True)  108 us
    reduce_scatter x1, waiting for transfers between devices, shards(): lax.psum_scatter(partial_grad, 'dp', scatter_dimension=1, tiled=True)  104 us
    psum x5, waiting for transfers between devices, refine_group(): lax.psum(inner_gram(iterate).astype(jnp.bfloat16), 'group')  99 us
    psum x1, waiting for transfers between devices, shards(): subspace = lax.psum(subspace_terms, 'dp')  95.1 us
    all_gather x1, waiting for transfers between devices, shards(): new_weight = lax.all_gather(updated, 'dp', axis=1, tiled=True)  50.5 us
    psum x1, waiting for transfers between devices, shards(): lax.psum(matmul(old_basis.T, grad_block).astype(jnp.bfloat16), 'group')  20.7 us
    dot_general x8, matrix products, matmul(): return jnp.dot(left, right, precision=HIGHEST)  16.8 us
    dot_general x1, matrix products, shards(): lax.dot_general(inputs, lax.all_gather(grad_out, 'group', axis=0, tiled=T...  14.6 us
  transfers between devices with their start and end apart: 10, of which 10 were waited for; matrix products, arithmetic and copies ran while one was open for 2% of the time, Pallas kernels for 0%

commit v1 on v0

--- a/solution.py
+++ b/solution.py
@@ -50,7 +50,21 @@
     col_offset = lax.axis_index("dp") * col_count
     own_cols = lax.dynamic_slice_in_dim(weight, col_offset, col_count, 1).astype(jnp.float32)
     updated = (own_cols - matmul(old_basis, direction)).astype(jnp.bfloat16)
-    new_weight = lax.all_gather(updated, "dp", axis=1, tiled=True)
+    ways, here, hop = (lax.axis_size("dp"), lax.axis_index("dp"), updated.shape[1])
+    dims = [n * ways if d == 1 else n for d, n in enumerate(updated.shape)]
+    full = lax.dynamic_update_slice_in_dim(
+        jnp.zeros(dims, updated.dtype), updated, here * hop, axis=1
+    )
+    going_up = going_down = updated
+    for far in range(1, ways // 2 + 1):
+        going_up = lax.ppermute(going_up, "dp", [(d, (d + 1) % ways) for d in range(ways)])
+        full = lax.dynamic_update_slice_in_dim(full, going_up, (here - far) % ways * hop, axis=1)
+        if 2 * far < ways:
+            going_down = lax.ppermute(going_down, "dp", [(d, (d - 1) % ways) for d in range(ways)])
+            full = lax.dynamic_update_slice_in_dim(
+                full, going_down, (here + far) % ways * hop, axis=1
+            )
+    new_weight = full
     subspace_terms = matmul(grad_block, projected.T)
     subspace = lax.psum(subspace_terms, "dp")
     new_basis = refine_group(subspace)

time: 559 us -> 524 us (0.937)
  waiting for transfers between devices: 478 us -> 401 us
  starting transfers between devices: 0.59 us -> 28 us
  local copies, waits for them, and re-layouts: 10.6 us -> 26.3 us
    all_gather x1 -> x0, waiting for transfers between devices: 50.5 us -> none  [shards(): new_weight = lax.all_gather(updated, 'dp', axis=1, tiled=True)]
    psum x5, waiting for transfers between devices: 99 us -> 70.1 us  [refine_group(): lax.psum(inner_gram(iterate).astype(jnp.bfloat16), 'group')]
    ppermute x0 -> x15, starting transfers between devices: none -> 27.6 us  [the longest x7 27.2 us: shards(): lax.ppermute(going_down, 'dp', [(d, (d - 1) % ways) for d in range(ways)])]
    dynamic_update_slice x0 -> x16, local copies, waits for them, and re-layouts: none -> 11.6 us  [the longest x8 5.81 us: shards(): lax.dynamic_update_slice_in_dim(full, going_up, (here - far) % ways * hop...]
    ppermute x0 -> x15, local copies, waits for them, and re-layouts: none -> 9.16 us  [the longest x8 5.14 us: shards(): lax.ppermute(going_up, 'dp', [(d, (d + 1) % ways) for d in range(ways)])]
    unnamed x14 -> x13, local copies, waits for them, and re-layouts: 9.66 us -> 1.87 us
    ppermute x0 -> x15, waiting for transfers between devices: none -> 7.39 us  [the longest x8 7.38 us: shards(): lax.ppermute(going_up, 'dp', [(d, (d + 1) % ways) for d in range(ways)])]
  transfers between devices with their start and end apart: 10 -> 24, of which waited for: 10 -> 11; matrix products, arithmetic and copies ran while one was open for 2% -> 10% of each run, Pallas kernels for 0% -> 0%
where the time goes in v1:
time: 524 us; the launch traced here: 523 us
  waiting for transfers between devices  401 us (77%)
  matrix products  44.6 us (9%)
  starting transfers between devices  28 us (5%)
  local copies, waits for them, and re-layouts  26.3 us (5%)
  between operations  15.2 us (3%)
  blocking collectives  5.54 us (1%)
    all_gather x1, waiting for transfers between devices, shards(): lax.all_gather(grad_out, 'group', axis=0, tiled=True)  108 us
    reduce_scatter x1, waiting for transfers between devices, shards(): lax.psum_scatter(partial_grad, 'dp', scatter_dimension=1, tiled=True)  104 us
    psum x1, waiting for transfers between devices, shards(): subspace = lax.psum(subspace_terms, 'dp')  90.5 us
    psum x5, waiting for transfers between devices, refine_group(): lax.psum(inner_gram(iterate).astype(jnp.bfloat16), 'group')  70.1 us
    ppermute x7, starting transfers between devices, shards(): lax.ppermute(going_down, 'dp', [(d, (d - 1) % ways) for d in range(ways)])  27.2 us
    psum x1, waiting for transfers between devices, shards(): lax.psum(matmul(old_basis.T, grad_block).astype(jnp.bfloat16), 'group')  20.7 us
    dot_general x8, matrix products, matmul(): return jnp.dot(left, right, precision=HIGHEST)  15.9 us
    dot_general x1, matrix products, shards(): lax.dot_general(inputs, lax.all_gather(grad_out, 'group', axis=0, tiled=T...  14.6 us
  transfers between devices with their start and end apart: 24, of which 11 were waited for; matrix products, arithmetic and copies ran while one was open for 10% of the time, Pallas kernels for 0%

profile of v1, /device:TPU:0, one launch (start us, length us, event | category | flops | bytes accessed | tf_op | source)
XLA Modules:
  0.0 523.3 jit_solution(14110787422751220477)
XLA Ops:
  8.0 108.3 %all-gather.2.cloned.1.call-done = bf16[2048,2048]{1,0:T(8,128)(2,1)} async-done(((bf16[1024,2048]{1,0:T(8,128)(2,1)}), bf16[2048,2048]{1,0:T(8,128)(2,1)}) %all-gather.2.cloned.1.call-update) | async-done | bytes 8388624 | tf_op jit(solution)/shard_map/all_gather | solution.py:34
  116.3 14.6 %fusion.21 = f32[1024,2048]{1,0:T(8,128)} fusion(bf16[2048,1024]{1,0:T(8,128)(2,1)} %param.6, bf16[2048,2048]{1,0:T(8,128)(2,1)} %all-gather.2.cloned.1.call-done), kind=kOutput, calls=%fused_computation.54 | convolution fusion | flops 8589934592 | bytes 20971520 | tf_op jit(solution)/shard_map/dot_general | solution.py:32
  131.0 103.7 %reduce-scatter.2.cloned.1.call-done = f32[1024,128]{1,0:T(8,128)} async-done(((f32[1024,2048]{1,0:T(8,128)}), f32[1024,128]{1,0:T(8,128)}) %reduce-scatter.2.cloned.1.call-update) | async-done | bytes 524304 | tf_op jit(solution)/shard_map/reduce_scatter | solution.py:38
  234.6 2.7 fusion.7
  237.4 20.7 %all-reduce.8.cloned.1.call-done = bf16[256,128]{0,1:T(8,128)(2,1)} async-done(((bf16[256,128]{0,1:T(8,128)(2,1)}), bf16[256,128]{0,1:T(8,128)(2,1)}) %all-reduce.8.cloned.1.call-update) | async-done | bytes 65552 | tf_op jit(solution)/shard_map/psum | solution.py:39
  258.1 2.6 fusion.22
  263.5 3.3 collective-permute-start.1
  266.7 90.5 %all-reduce.10.cloned.1.call-done = f32[1024,256]{1,0:T(8,128)} async-done(((f32[1024,256]{1,0:T(8,128)}), f32[1024,256]{1,0:T(8,128)}) %all-reduce.10.cloned.1.call-update) | async-done | bytes 1048592 | tf_op jit(solution)/shard_map/psum | solution.py:69
  357.2 2.1 multiply_reduce_fusion
  359.3 5.5 %psum.58 = f32[]{:T(128)} all-reduce(f32[]{:T(128)} %multiply_reduce_fusion), channel_id=1, replica_groups=mesh['dp'=16,'group'=2] {'group'}, use_global_device_ids=true, to_apply=%region_4.5 | all-reduce | flops 1 | bytes 8 | tf_op jit(solution)/shard_map/psum | solution.py:23
  365.6 4.1 convolution_convert_fusion.4
  371.7 2.5 broadcast_in_dim.3
  375.5 4.2 collective-permute-start.3
  379.7 11.7 %all-reduce.12.cloned.1.call-done = bf16[256,256]{1,0:T(8,128)(2,1)} async-done(((bf16[256,256]{1,0:T(8,128)(2,1)}), bf16[256,256]{1,0:T(8,128)(2,1)}) %all-reduce.12.cloned.1.call-update) | async-done | bytes 131088 | tf_op jit(solution)/shard_map/psum | solution.py:26
  391.4 2.3 fusion.4
  393.7 2.5 convolution_convert_fusion.3
  399.1 4.4 collective-permute-start.5
  403.5 14.4 %all-reduce.14.cloned.1.call-done = bf16[256,256]{1,0:T(8,128)(2,1)} async-done(((bf16[256,256]{1,0:T(8,128)(2,1)}), bf16[256,256]{1,0:T(8,128)(2,1)}) %all-reduce.14.cloned.1.call-update) | async-done | bytes 131088 | tf_op jit(solution)/shard_map/psum | solution.py:26
  417.9 1.5 fusion.3
  419.4 2.5 convolution_convert_fusion.2
  425.8 4.4 collective-permute-start.7
  430.2 13.4 %all-reduce.16.cloned.1.call-done = bf16[256,256]{1,0:T(8,128)(2,1)} async-done(((bf16[256,256]{1,0:T(8,128)(2,1)}), bf16[256,256]{1,0:T(8,128)(2,1)}) %all-reduce.16.cloned.1.call-update) | async-done | bytes 131088 | tf_op jit(solution)/shard_map/psum | solution.py:26
  443.6 1.5 fusion.2
  445.1 2.5 convolution_convert_fusion.1
  450.3 3.2 collective-permute-start.9
  453.5 15.8 %all-reduce.18.cloned.1.call-done = bf16[256,256]{1,0:T(8,128)(2,1)} async-done(((bf16[256,256]{1,0:T(8,128)(2,1)}), bf16[256,256]{1,0:T(8,128)(2,1)}) %all-reduce.18.cloned.1.call-update) | async-done | bytes 131088 | tf_op jit(solution)/shard_map/psum | solution.py:26
  470.9 2.5 convolution_convert_fusion
  477.1 3.2 collective-permute-start.11
  480.3 14.8 %all-reduce.20.cloned.1.call-done = bf16[256,256]{1,0:T(8,128)(2,1)} async-done(((bf16[256,256]{1,0:T(8,128)(2,1)}), bf16[256,256]{1,0:T(8,128)(2,1)}) %all-reduce.20.cloned.1.call-update) | async-done | bytes 131088 | tf_op jit(solution)/shard_map/psum | solution.py:26
  495.1 2.5 fusion
  499.7 4.5 collective-permute-start.13
  509.9 6.0 %collective-permute-done.14 = bf16[1024,128]{0,1:T(8,128)(2,1)S(1)} collective-permute-done((bf16[1024,128]{0,1:T(8,128)(2,1)S(1)}, bf16[1024,128]{0,1:T(8,128)(2,1)S(1)}, u32[]{:S(2)}, u32[]{:S(2)}) %collective-permute-start.14) | collective-permute-done | bytes 262176 | tf_op jit(solution)/shard_map/ppermute | solution.py:60
  (89 shorter events, 29.7 us)
Async XLA Ops:
  7.2 227.5 %copy-start = (f32[1024,256]{1,0:T(8,128)S(1)}, f32[1024,256]{1,0:T(8,128)}, u32[]{:S(2)}) copy-start(f32[1024,256]{1,0:T(8,128)} %param.9) | copy-start | bytes 3145732
  7.2 109.1 %all-gather.2.cloned.1.call-start = ((), (), s32[]{:S(2)}) async-start(), calls=%async_computation.1 | async-start | bytes 12582912 | tf_op jit(solution)/shard_map/all_gather | solution.py:34
  7.9 226.7 %reduce-scatter.2.cloned.1.call-start = ((), (), s32[]{:S(2)}) async-start(), calls=%async_computation.2 | async-start | bytes 8912896 | tf_op jit(solution)/shard_map/reduce_scatter | solution.py:38
  130.9 130.9 %copy-start.2 = (f32[256,128]{1,0:T(8,128)S(1)}, f32[256,128]{1,0:T(8,128)}, u32[]{:S(2)}) copy-start(f32[256,128]{1,0:T(8,128)} %param.10) | copy-start | bytes 393220
  130.9 131.0 %copy-start.3 = (f32[256,128]{1,0:T(8,128)S(1)}, f32[256,128]{1,0:T(8,128)}, u32[]{:S(2)}) copy-start(f32[256,128]{1,0:T(8,128)} %param.11) | copy-start | bytes 393220
  130.9 127.2 %all-reduce.8.cloned.1.call-start = ((), (), s32[]{:S(2)}) async-start(), calls=%async_computation.3 | async-start | bytes 131072 | tf_op jit(solution)/shard_map/psum | solution.py:39
  237.4 119.8 %all-reduce.10.cloned.1.call-start = ((), (), s32[]{:S(2)}) async-start(), calls=%async_computation.4 | async-start | bytes 2097152 | tf_op jit(solution)/shard_map/psum | solution.py:69
  258.1 4.1 copy-start.1
  260.7 130.6 %all-reduce.12.cloned.1.call-start = ((), (), s32[]{:S(2)}) async-start(), calls=%async_computation.5 | async-start | bytes 262144 | tf_op jit(solution)/shard_map/psum | solution.py:26
  263.5 112.0 %collective-permute-start.1 = (bf16[1024,128]{0,1:T(8,128)(2,1)S(1)}, bf16[1024,128]{0,1:T(8,128)(2,1)S(1)}, u32[]{:S(2)}, u32[]{:S(2)}) collective-permute-start(bf16[1024,128]{0,1:T(8,128)(2,1)S(1)} %fusion.6), channel_id=1, source_target_pairs={{0,30},{2,0},{4,2},{6,4},{8,6},{10,8},{12,10},{14,12},{16,14},{18,... | collective-permute-start | bytes 786440 | tf_op jit(solution)/shard_map/ppermute | solution.py:63
  359.3 15.7 %collective-permute-start = (bf16[1024,128]{0,1:T(8,128)(2,1)S(1)}, bf16[1024,128]{0,1:T(8,128)(2,1)S(1)}, u32[]{:S(2)}, u32[]{:S(2)}) collective-permute-start(bf16[1024,128]{0,1:T(8,128)(2,1)S(1)} %fusion.6), channel_id=1, source_target_pairs={{0,2},{2,4},{4,6},{6,8},{8,10},{10,12},{12,14},{14,16},{16,18},{18... | collective-permute-start | bytes 786440 | tf_op jit(solution)/shard_map/ppermute | solution.py:60
  369.7 48.2 %all-reduce.14.cloned.1.call-start = ((), (), s32[]{:S(2)}) async-start(), calls=%async_computation.6 | async-start | bytes 262144 | tf_op jit(solution)/shard_map/psum | solution.py:26
  375.2 22.7 %collective-permute-start.2 = (bf16[1024,128]{0,1:T(8,128)(2,1)S(1)}, bf16[1024,128]{0,1:T(8,128)(2,1)}, u32[]{:S(2)}, u32[]{:S(2)}) collective-permute-start(bf16[1024,128]{0,1:T(8,128)(2,1)S(1)} %collective-permute-done), channel_id=1, source_target_pairs={{0,2},{2,4},{4,6},{6,8},{8,10},{10,12},{12,14},{14,16},{16,18},{18... | collective-permute-start | bytes 786440 | tf_op jit(solution)/shard_map/ppermute | solution.py:60
  375.5 23.6 %collective-permute-start.3 = (bf16[1024,128]{0,1:T(8,128)(2,1)S(1)}, bf16[1024,128]{0,1:T(8,128)(2,1)}, u32[]{:S(2)}, u32[]{:S(2)}) collective-permute-start(bf16[1024,128]{0,1:T(8,128)(2,1)S(1)} %collective-permute-done.1), channel_id=1, source_target_pairs={{0,30},{2,0},{4,2},{6,4},{8,6},{10,8},{12,10},{14,12},{16,14},{18,... | collective-permute-start | bytes 786440 | tf_op jit(solution)/shard_map/ppermute | solution.py:63
  396.2 47.4 %all-reduce.16.cloned.1.call-start = ((), (), s32[]{:S(2)}) async-start(), calls=%async_computation.7 | async-start | bytes 262144 | tf_op jit(solution)/shard_map/psum | solution.py:26
  399.0 25.6 %collective-permute-start.4 = (bf16[1024,128]{0,1:T(8,128)(2,1)}, bf16[1024,128]{0,1:T(8,128)(2,1)}, u32[]{:S(2)}, u32[]{:S(2)}) collective-permute-start(bf16[1024,128]{0,1:T(8,128)(2,1)} %collective-permute-done.2), channel_id=1, source_target_pairs={{0,2},{2,4},{4,6},{6,8},{8,10},{10,12},{12,14},{14,16},{16,18},{18... | collective-permute-start | bytes 786440 | tf_op jit(solution)/shard_map/ppermute | solution.py:60
  399.1 26.7 %collective-permute-start.5 = (bf16[1024,128]{0,1:T(8,128)(2,1)}, bf16[1024,128]{0,1:T(8,128)(2,1)}, u32[]{:S(2)}, u32[]{:S(2)}) collective-permute-start(bf16[1024,128]{0,1:T(8,128)(2,1)} %collective-permute-done.3), channel_id=1, source_target_pairs={{0,30},{2,0},{4,2},{6,4},{8,6},{10,8},{12,10},{14,12},{16,14},{18,... | collective-permute-start | bytes 786440 | tf_op jit(solution)/shard_map/ppermute | solution.py:63
  421.9 47.4 %all-reduce.18.cloned.1.call-start = ((), (), s32[]{:S(2)}) async-start(), calls=%async_computation.8 | async-start | bytes 262144 | tf_op jit(solution)/shard_map/psum | solution.py:26
  425.7 27.8 %collective-permute-start.6 = (bf16[1024,128]{0,1:T(8,128)(2,1)}, bf16[1024,128]{0,1:T(8,128)(2,1)}, u32[]{:S(2)}, u32[]{:S(2)}) collective-permute-start(bf16[1024,128]{0,1:T(8,128)(2,1)} %collective-permute-done.4), channel_id=1, source_target_pairs={{0,2},{2,4},{4,6},{6,8},{8,10},{10,12},{12,14},{14,16},{16,18},{18... | collective-permute-start | bytes 786440 | tf_op jit(solution)/shard_map/ppermute | solution.py:60
  425.8 24.5 %collective-permute-start.7 = (bf16[1024,128]{0,1:T(8,128)(2,1)}, bf16[1024,128]{0,1:T(8,128)(2,1)}, u32[]{:S(2)}, u32[]{:S(2)}) collective-permute-start(bf16[1024,128]{0,1:T(8,128)(2,1)} %collective-permute-done.5), channel_id=1, source_target_pairs={{0,30},{2,0},{4,2},{6,4},{8,6},{10,8},{12,10},{14,12},{16,14},{18,... | collective-permute-start | bytes 786440 | tf_op jit(solution)/shard_map/ppermute | solution.py:63
  447.7 47.4 %all-reduce.20.cloned.1.call-start = ((), (), s32[]{:S(2)}) async-start(), calls=%async_computation.9 | async-start | bytes 262144 | tf_op jit(solution)/shard_map/psum | solution.py:26
  450.3 26.8 %collective-permute-start.9 = (bf16[1024,128]{0,1:T(8,128)(2,1)}, bf16[1024,128]{0,1:T(8,128)(2,1)S(1)}, u32[]{:S(2)}, u32[]{:S(2)}) collective-permute-start(bf16[1024,128]{0,1:T(8,128)(2,1)} %collective-permute-done.7), channel_id=1, source_target_pairs={{0,30},{2,0},{4,2},{6,4},{8,6},{10,8},{12,10},{14,12},{16,14},{18,... | collective-permute-start | bytes 786440 | tf_op jit(solution)/shard_map/ppermute | solution.py:63
  453.5 26.8 %collective-permute-start.8 = (bf16[1024,128]{0,1:T(8,128)(2,1)}, bf16[1024,128]{0,1:T(8,128)(2,1)}, u32[]{:S(2)}, u32[]{:S(2)}) collective-permute-start(bf16[1024,128]{0,1:T(8,128)(2,1)} %collective-permute-done.6), channel_id=1, source_target_pairs={{0,2},{2,4},{4,6},{6,8},{8,10},{10,12},{12,14},{14,16},{16,18},{18... | collective-permute-start | bytes 786440 | tf_op jit(solution)/shard_map/ppermute | solution.py:60
  477.1 22.6 %collective-permute-start.11 = (bf16[1024,128]{0,1:T(8,128)(2,1)S(1)}, bf16[1024,128]{0,1:T(8,128)(2,1)S(1)}, u32[]{:S(2)}, u32[]{:S(2)}) collective-permute-start(bf16[1024,128]{0,1:T(8,128)(2,1)S(1)} %collective-permute-done.9), channel_id=1, source_target_pairs={{0,30},{2,0},{4,2},{6,4},{8,6},{10,8},{12,10},{14,12},{16,14},{18,... | collective-permute-start | bytes 786440 | tf_op jit(solution)/shard_map/ppermute | solution.py:63
  480.3 18.4 %collective-permute-start.10 = (bf16[1024,128]{0,1:T(8,128)(2,1)}, bf16[1024,128]{0,1:T(8,128)(2,1)S(1)}, u32[]{:S(2)}, u32[]{:S(2)}) collective-permute-start(bf16[1024,128]{0,1:T(8,128)(2,1)} %collective-permute-done.8), channel_id=1, source_target_pairs={{0,2},{2,4},{4,6},{6,8},{8,10},{10,12},{12,14},{14,16},{16,18},{18... | collective-permute-start | bytes 786440 | tf_op jit(solution)/shard_map/ppermute | solution.py:60
  498.7 8.6 %collective-permute-start.12 = (bf16[1024,128]{0,1:T(8,128)(2,1)S(1)}, bf16[1024,128]{0,1:T(8,128)(2,1)S(1)}, u32[]{:S(2)}, u32[]{:S(2)}) collective-permute-start(bf16[1024,128]{0,1:T(8,128)(2,1)S(1)} %collective-permute-done.10), channel_id=1, source_target_pairs={{0,2},{2,4},{4,6},{6,8},{8,10},{10,12},{12,14},{14,16},{16,18},{18... | collective-permute-start | bytes 786440 | tf_op jit(solution)/shard_map/ppermute | solution.py:60
  499.7 8.6 %collective-permute-start.13 = (bf16[1024,128]{0,1:T(8,128)(2,1)S(1)}, bf16[1024,128]{0,1:T(8,128)(2,1)S(1)}, u32[]{:S(2)}, u32[]{:S(2)}) collective-permute-start(bf16[1024,128]{0,1:T(8,128)(2,1)S(1)} %collective-permute-done.11), channel_id=1, source_target_pairs={{0,30},{2,0},{4,2},{6,4},{8,6},{10,8},{12,10},{14,12},{16,14},{18,... | collective-permute-start | bytes 786440 | tf_op jit(solution)/shard_map/ppermute | solution.py:63
  507.4 8.5 %collective-permute-start.14 = (bf16[1024,128]{0,1:T(8,128)(2,1)S(1)}, bf16[1024,128]{0,1:T(8,128)(2,1)S(1)}, u32[]{:S(2)}, u32[]{:S(2)}) collective-permute-start(bf16[1024,128]{0,1:T(8,128)(2,1)S(1)} %collective-permute-done.12), channel_id=1, source_target_pairs={{0,2},{2,4},{4,6},{6,8},{8,10},{10,12},{12,14},{14,16},{16,18},{18... | collective-permute-start | bytes 786440 | tf_op jit(solution)/shard_map/ppermute | solution.py:60
Sparse Core Ops, SparseCore 0:
  9.5 106.6 all-gather.1
  131.0 103.5 reduce-scatter.1
  237.5 20.5 all-reduce.7
  262.0 95.1 all-reduce.9
  369.8 21.5 all-reduce.11
  396.3 21.5 all-reduce.13
  422.1 21.5 all-reduce.15
  447.8 21.5 all-reduce.17
  473.5 21.5 all-reduce.19
